TPU v7x, 512 devices: a whole 4x8x8 slice. The times are simulated.
512 devices in a mesh: ind: 64 (over y, z), snp: 8 (over x, core).
Axes of the slice: x: 4, y: 8, z: 8, core: 2. Of those that a mesh axis runs over, the one named last changes fastest.
Arguments:
- genotypes: int32 [4096, 16384], P('ind', 'snp'), may hold values from 0 to 2
- observed: int32 [4096, 16384], P('ind', 'snp'), may hold values from 0 to 1
- ancestry: float32 [4096, 32], P('ind'), may hold values from 0.018 to 54.6, as said below
- freqs: float32 [16384, 32], P(('snp', 'ind')), may hold values from 0.05 to 0.95
Outputs:
- ancestry_out: float32 [4096, 32], P('ind')
- freqs_out: float32 [16384, 32], P(('snp', 'ind'))
Inputs may be any that keep to these rules, and one draw needn't show every extreme that they name: `ancestry`: positive weights.
All inputs are finite; a program needn't handle non-finite values.
Results may differ from a plain program's by a relative error of at most 0.0003.
Values sent between devices are 32-bit elements; how exact they have to be, the bound alone decides.
No kernel may reach another device: no remote copies, remote signals or barrier semaphores. Data moves between devices by JAX's collectives and lax.ppermute only.
A program may use at most 64 MiB of HBM per device.

v0:
```python
import jax
import jax.numpy as jnp
from jax import lax
from jax.sharding import Mesh
from jax.sharding import PartitionSpec as P

STEPS = 3
clip_low = 1e-05
high = lax.Precision.HIGHEST
IND_AXES = ("yh", "yl", "z")
SNP_AXES = ("x", "c")
ROW_GROUP = ("yl", "z")
COL_GROUP = ("c", "x", "yh")


def doubling_sum(value, axes):
    for name in axes:
        size = lax.axis_size(name)
        step = 1
        while step < size:
            pairs = [(j, j ^ step) for j in range(size)]
            value = value + lax.ppermute(value, name, pairs)
            step *= 2
    return value


def per_device(genotypes, observed, ancestry, freqs):
    quarter = lax.axis_size("yh")
    geno = genotypes.astype(jnp.float32)
    seen = observed.astype(jnp.float32)
    counts = jnp.stack([seen * geno, seen * (2.0 - geno)])
    counts = lax.all_to_all(counts, "yh", 2, 1, tiled=True)
    hits, misses = (counts[0], counts[1])
    own_rows = ancestry.shape[0]
    own_snps = freqs.shape[0]
    q_own = ancestry / jnp.sum(ancestry, axis=1, keepdims=True)
    q_zero = lax.all_gather(q_own, "yh", axis=0, tiled=True)
    f_zero = lax.all_gather(freqs, ROW_GROUP, axis=0, tiled=True)

    def em_map(q_rows, f_state):
        prob = jnp.dot(q_rows, f_state.T, precision=high, preferred_element_type=jnp.float32)
        ratio_a = hits / prob
        ratio_b = misses / (1.0 - prob)
        sum_a = jnp.dot(ratio_a, f_state, precision=high, preferred_element_type=jnp.float32)
        sum_b = jnp.dot(ratio_b, 1.0 - f_state, precision=high, preferred_element_type=jnp.float32)
        c_part = lax.dot_general(
            ratio_a,
            q_rows,
            (((0,), (0,)), ((), ())),
            precision=high,
            preferred_element_type=jnp.float32,
        )
        d_part = lax.dot_general(
            ratio_b,
            q_rows,
            (((0,), (0,)), ((), ())),
            precision=high,
            preferred_element_type=jnp.float32,
        )
        q_sum = doubling_sum(sum_a + sum_b, COL_GROUP)
        cd_total = doubling_sum(jnp.concatenate([c_part, d_part], axis=1), ROW_GROUP)
        q_next = q_rows * q_sum
        q_next = q_next / jnp.sum(q_next, axis=1, keepdims=True)
        width = f_state.shape[1]
        c_total, d_total = (cd_total[:, :width], cd_total[:, width:])
        f_next = f_state * c_total / (f_state * c_total + (1.0 - f_state) * d_total)
        return (q_next, f_next)

    for step in range(STEPS):
        q_one, f_one = em_map(q_zero, f_zero)
        q_two, f_two = em_map(q_one, f_one)
        rq = q_one - q_zero
        rf = f_one - f_zero
        vq = q_two - 2.0 * q_one + q_zero
        vf = f_two - 2.0 * f_one + f_zero
        q_parts = doubling_sum(jnp.stack([jnp.sum(rq * rq), jnp.sum(vq * vq)]), ROW_GROUP)
        f_parts = doubling_sum(jnp.stack([jnp.sum(rf * rf), jnp.sum(vf * vf)]), COL_GROUP)
        first = q_parts[0] + f_parts[0]
        second = q_parts[1] + f_parts[1]
        alpha = -jnp.sqrt(first / (second + 1e-20))
        q_ext = jnp.clip(q_zero - 2.0 * alpha * rq + alpha * alpha * vq, clip_low, 1.0 - clip_low)
        q_zero = q_ext / jnp.sum(q_ext, axis=1, keepdims=True)
        f_zero = jnp.clip(f_zero - 2.0 * alpha * rf + alpha * alpha * vf, clip_low, 1.0 - clip_low)
    q_final = lax.dynamic_slice_in_dim(q_zero, lax.axis_index("yh") * own_rows, own_rows, 0)
    f_index = lax.axis_index("yl") * lax.axis_size("z") + lax.axis_index("z")
    f_final = lax.dynamic_slice_in_dim(f_zero, f_index * own_snps, own_snps, 0)
    del quarter
    return (q_final, f_final)


def solution(mesh):
    ind_size = mesh.shape["ind"]
    snp_size = mesh.shape["snp"]
    quarter = 4
    lanes = ind_size // quarter
    view = Mesh(
        mesh.devices.reshape(quarter, 2, lanes // 2, snp_size // 2, 2), ("yh", "yl", "z", "x", "c")
    )
    in_specs = (
        P(IND_AXES, SNP_AXES),
        P(IND_AXES, SNP_AXES),
        P(IND_AXES, None),
        P(SNP_AXES + IND_AXES, None),
    )
    out_specs = (P(IND_AXES, None), P(SNP_AXES + IND_AXES, None))
    return jax.shard_map(
        per_device, mesh=view, in_specs=in_specs, out_specs=out_specs, check_vma=False
    )
```

profile of v0, /device:TPU:56, one launch (start us, length us, event | category | flops | bytes accessed | tf_op | source)
XLA Modules:
  0.0 610.7 jit_solution(14223782295887713590)
XLA Ops:
  9.1 7.0 %all-to-all-start = ((f32[4,1,65536]{2,1,0:T(1,128)}), f32[4,1,65536]{2,1,0:T(1,128)S(1)}, u32[]{:S(2)}, u32[]{:S(2)}) async-start(f32[4,1,65536]{2,1,0:T(1,128)} %reshape.50), calls=%async_computation | async-start | bytes 2097152 | tf_op jit(solution)/shard_map/all_to_all | solution.py:32
  16.1 32.8 %all-gather = f32[4,64,32]{1,2,0:T(8,128)S(1)} all-gather(f32[1,64,32]{1,2,0:T(8,128)S(1)} %divide_bitcast_fusion), channel_id=1, replica_groups=mesh['yh'=4,'yl'=2,'z'=8,'x'=4,'c'=2] {'yh'}, dimensions={0}, use_global_device_ids=true | all-gather | bytes 40960 | tf_op jit(solution)/shard_map/all_gather | solution.py:37
  49.1 40.7 %all_gather.7 = f32[512,32]{1,0:T(8,128)S(1)} all-gather(f32[32,32]{1,0:T(8,128)S(1)} %copy-done.1), channel_id=1, replica_groups=mesh['yh'=4,'yl'=2,'z'=8,'x'=4,'c'=2] {'yl','z'}, dimensions={0}, use_global_device_ids=true | all-gather | bytes 69632 | tf_op jit(solution)/shard_map/all_gather | solution.py:38
  90.4 3.7 reduce
  107.3 3.4 collective-permute-start.1
  113.1 4.9 collective-permute-start.2
  122.9 4.5 collective-permute-done.3
  127.4 5.4 collective-permute-start.4
  137.2 3.6 collective-permute-done.7
  143.5 9.4 %collective-permute-done.8 = f32[512,64]{0,1:T(8,128)S(1)} collective-permute-done((f32[512,64]{0,1:T(8,128)S(1)}, f32[512,64]{0,1:T(8,128)S(1)}, u32[]{:S(2)}, u32[]{:S(2)}) %collective-permute-start.8) | collective-permute-done | bytes 131104 | tf_op jit(solution)/shard_map/ppermute | solution.py:22
  160.2 3.4 collective-permute-start.10
  166.0 4.9 collective-permute-start.11
  175.5 4.5 collective-permute-done.12
  180.0 4.3 collective-permute-start.13
  184.3 4.4 collective-permute-start.19
  191.8 3.9 collective-permute-start.14
  199.2 4.1 collective-permute-start.15
  203.6 3.8 collective-permute-start.21
  211.4 3.8 collective-permute-done.16
  215.2 5.9 collective-permute-start.17
  221.1 3.4 collective-permute-done.17
  231.3 3.4 collective-permute-start.23
  238.0 4.9 collective-permute-start.24
  247.3 3.9 collective-permute-done.25
  253.8 6.8 %collective-permute-done.26 = f32[2]{0:T(128)S(1)} collective-permute-done((f32[2]{0:T(128)S(1)}, f32[2]{0:T(128)S(1)}, u32[]{:S(2)}, u32[]{:S(2)}) %collective-permute-start.26) | collective-permute-done | bytes 40 | tf_op jit(solution)/shard_map/ppermute | solution.py:22
  276.3 3.4 collective-permute-start.28
  282.1 4.9 collective-permute-start.29
  291.4 4.9 collective-permute-done.30
  296.3 4.1 collective-permute-start.31
  308.9 10.6 %collective-permute-start.35 = (f32[512,64]{0,1:T(8,128)S(1)}, f32[512,64]{0,1:T(8,128)S(1)}, u32[]{:S(2)}, u32[]{:S(2)}) collective-permute-start(f32[512,64]{0,1:T(8,128)S(1)} %add.406), channel_id=1, source_target_pairs={{0,32},{8,40},{16,48},{24,56},{32,0},{40,8},{48,16},{56,24},{1,33}... | collective-permute-start | bytes 393224 | tf_op jit(solution)/shard_map/ppermute | solution.py:22
  329.7 3.4 collective-permute-start.37
  335.5 4.9 collective-permute-start.38
  345.2 4.3 collective-permute-done.39
  349.6 5.6 collective-permute-start.40
  361.9 4.2 collective-permute-start.41
  369.5 3.8 collective-permute-start.42
  374.5 9.2 %collective-permute-start.48 = (f32[512,64]{0,1:T(8,128)S(1)}, f32[512,64]{0,1:T(8,128)S(1)}, u32[]{:S(2)}, u32[]{:S(2)}) collective-permute-start(f32[512,64]{0,1:T(8,128)S(1)} %add.422), channel_id=1, source_target_pairs={{0,32},{8,40},{16,48},{24,56},{32,0},{40,8},{48,16},{56,24},{1,33}... | collective-permute-start | bytes 393224 | tf_op jit(solution)/shard_map/ppermute | solution.py:22
  387.0 4.4 collective-permute-done.43
  393.4 7.4 %collective-permute-done.44 = f32[2]{0:T(128)S(1)} collective-permute-done((f32[2]{0:T(128)S(1)}, f32[2]{0:T(128)S(1)}, u32[]{:S(2)}, u32[]{:S(2)}) %collective-permute-start.44) | collective-permute-done | bytes 40 | tf_op jit(solution)/shard_map/ppermute | solution.py:22
  407.5 3.4 collective-permute-start.50
  414.2 4.9 collective-permute-start.51
  423.3 4.2 collective-permute-done.52
  427.5 5.0 collective-permute-start.53
  432.5 4.4 collective-permute-done.53
  451.1 3.4 collective-permute-start.55
  456.9 4.9 collective-permute-start.56
  466.3 4.6 collective-permute-done.57
  470.9 5.0 collective-permute-start.58
  475.9 4.8 collective-permute-start.61
  481.0 5.5 collective-permute-done.61
  488.5 8.8 %collective-permute-done.62 = f32[512,64]{0,1:T(8,128)S(1)} collective-permute-done((f32[512,64]{0,1:T(8,128)S(1)}, f32[512,64]{0,1:T(8,128)S(1)}, u32[]{:S(2)}, u32[]{:S(2)}) %collective-permute-start.62) | collective-permute-done | bytes 131104 | tf_op jit(solution)/shard_map/ppermute | solution.py:22
  504.6 3.4 collective-permute-start.64
  510.4 4.9 collective-permute-start.65
  519.8 4.6 collective-permute-done.66
  524.4 4.2 collective-permute-start.67
  536.9 3.9 collective-permute-start.68
  545.1 3.9 collective-permute-start.69
  556.2 4.4 collective-permute-done.70
  560.6 7.8 %collective-permute-start.71 = (f32[2]{0:T(128)S(1)}, f32[2]{0:T(128)S(1)}, u32[]{:S(2)}, u32[]{:S(2)}) collective-permute-start(f32[2]{0:T(128)S(1)} %add.456), channel_id=1, source_target_pairs={{0,32},{8,40},{16,48},{24,56},{32,0},{40,8},{48,16},{56,24},{1,33}... | collective-permute-start | bytes 32 | tf_op jit(solution)/shard_map/ppermute | solution.py:22
  576.7 3.4 collective-permute-start.77
  583.4 4.9 collective-permute-start.78
  592.2 4.4 collective-permute-done.79
  596.6 4.1 collective-permute-start.80
  600.8 5.2 collective-permute-done.80
  (271 shorter events, 226.7 us)
Async XLA Ops:
  9.1 80.8 %all-to-all-start = ((f32[4,1,65536]{2,1,0:T(1,128)}), f32[4,1,65536]{2,1,0:T(1,128)S(1)}, u32[]{:S(2)}, u32[]{:S(2)}) async-start(f32[4,1,65536]{2,1,0:T(1,128)} %reshape.50), calls=%async_computation | async-start | bytes 2097152 | tf_op jit(solution)/shard_map/all_to_all | solution.py:32
  98.4 6.9 %collective-permute-start.5 = (f32[512,64]{0,1:T(8,128)S(1)}, f32[512,64]{0,1:T(8,128)S(1)}, u32[]{:S(2)}, u32[]{:S(2)}) collective-permute-start(f32[512,64]{0,1:T(8,128)S(1)} %pad_maximum_fusion.1), channel_id=1, source_target_pairs={{0,64},{64,0},{1,65},{65,1},{2,66},{66,2},{3,67},{67,3},{4,68},{68... | collective-permute-start | bytes 393224 | tf_op jit(solution)/shard_map/ppermute | solution.py:22
  105.3 27.6 %collective-permute-start.6 = (f32[512,64]{0,1:T(8,128)S(1)}, f32[512,64]{0,1:T(8,128)S(1)}, u32[]{:S(2)}, u32[]{:S(2)}) collective-permute-start(f32[512,64]{0,1:T(8,128)S(1)} %fusion.41), channel_id=1, source_target_pairs={{0,8},{8,0},{16,24},{24,16},{32,40},{40,32},{48,56},{56,48},{1,9},... | collective-permute-start | bytes 393224 | tf_op jit(solution)/shard_map/ppermute | solution.py:22
  113.1 7.3 %collective-permute-start.2 = (f32[256,32]{0,1:T(8,128)S(1)}, f32[256,32]{0,1:T(8,128)S(1)}, u32[]{:S(2)}, u32[]{:S(2)}) collective-permute-start(f32[256,32]{0,1:T(8,128)S(1)} %add.362), channel_id=1, source_target_pairs={{0,4},{2,6},{4,0},{6,2},{1,5},{3,7},{5,1},{7,3},{8,12},{10,14},{12... | collective-permute-start | bytes 98312 | tf_op jit(solution)/shard_map/ppermute | solution.py:22
  120.4 7.0 %collective-permute-start.3 = (f32[256,32]{0,1:T(8,128)S(1)}, f32[256,32]{0,1:T(8,128)S(1)}, u32[]{:S(2)}, u32[]{:S(2)}) collective-permute-start(f32[256,32]{0,1:T(8,128)S(1)} %add.363), channel_id=1, source_target_pairs={{0,128},{128,0},{256,384},{384,256},{1,129},{129,1},{257,385},{385... | collective-permute-start | bytes 98312 | tf_op jit(solution)/shard_map/ppermute | solution.py:22
  127.4 9.7 %collective-permute-start.4 = (f32[256,32]{0,1:T(8,128)S(1)}, f32[256,32]{0,1:T(8,128)S(1)}, u32[]{:S(2)}, u32[]{:S(2)}) collective-permute-start(f32[256,32]{0,1:T(8,128)S(1)} %add.364), channel_id=1, source_target_pairs={{0,256},{128,384},{256,0},{384,128},{1,257},{129,385},{257,1},{385... | collective-permute-start | bytes 98312 | tf_op jit(solution)/shard_map/ppermute | solution.py:22
  132.9 7.9 %collective-permute-start.7 = (f32[512,64]{0,1:T(8,128)S(1)}, f32[512,64]{0,1:T(8,128)S(1)}, u32[]{:S(2)}, u32[]{:S(2)}) collective-permute-start(f32[512,64]{0,1:T(8,128)S(1)} %add.367), channel_id=1, source_target_pairs={{0,16},{8,24},{16,0},{24,8},{32,48},{40,56},{48,32},{56,40},{1,17}... | collective-permute-start | bytes 393224 | tf_op jit(solution)/shard_map/ppermute | solution.py:22
  140.8 12.1 %collective-permute-start.8 = (f32[512,64]{0,1:T(8,128)S(1)}, f32[512,64]{0,1:T(8,128)S(1)}, u32[]{:S(2)}, u32[]{:S(2)}) collective-permute-start(f32[512,64]{0,1:T(8,128)S(1)} %add.368), channel_id=1, source_target_pairs={{0,32},{8,40},{16,48},{24,56},{32,0},{40,8},{48,16},{56,24},{1,33}... | collective-permute-start | bytes 393224 | tf_op jit(solution)/shard_map/ppermute | solution.py:22
  158.2 26.0 %collective-permute-start.18 = (f32[512,64]{0,1:T(8,128)S(1)}, f32[512,64]{0,1:T(8,128)S(1)}, u32[]{:S(2)}, u32[]{:S(2)}) collective-permute-start(f32[512,64]{0,1:T(8,128)S(1)} %pad_maximum_fusion.2), channel_id=1, source_target_pairs={{0,64},{64,0},{1,65},{65,1},{2,66},{66,2},{3,67},{67,3},{4,68},{68... | collective-permute-start | bytes 393224 | tf_op jit(solution)/shard_map/ppermute | solution.py:22
  166.0 7.3 %collective-permute-start.11 = (f32[256,32]{0,1:T(8,128)S(1)}, f32[256,32]{0,1:T(8,128)S(1)}, u32[]{:S(2)}, u32[]{:S(2)}) collective-permute-start(f32[256,32]{0,1:T(8,128)S(1)} %add.373), channel_id=1, source_target_pairs={{0,4},{2,6},{4,0},{6,2},{1,5},{3,7},{5,1},{7,3},{8,12},{10,14},{12... | collective-permute-start | bytes 98312 | tf_op jit(solution)/shard_map/ppermute | solution.py:22
  173.3 6.7 %collective-permute-start.12 = (f32[256,32]{0,1:T(8,128)S(1)}, f32[256,32]{0,1:T(8,128)S(1)}, u32[]{:S(2)}, u32[]{:S(2)}) collective-permute-start(f32[256,32]{0,1:T(8,128)S(1)} %add.374), channel_id=1, source_target_pairs={{0,128},{128,0},{256,384},{384,256},{1,129},{129,1},{257,385},{385... | collective-permute-start | bytes 98312 | tf_op jit(solution)/shard_map/ppermute | solution.py:22
  180.0 9.7 %collective-permute-start.13 = (f32[256,32]{0,1:T(8,128)S(1)}, f32[256,32]{0,1:T(8,128)S(1)}, u32[]{:S(2)}, u32[]{:S(2)}) collective-permute-start(f32[256,32]{0,1:T(8,128)S(1)} %add.375), channel_id=1, source_target_pairs={{0,256},{128,384},{256,0},{384,128},{1,257},{129,385},{257,1},{385... | collective-permute-start | bytes 98312 | tf_op jit(solution)/shard_map/ppermute | solution.py:22
  184.3 11.5 %collective-permute-start.19 = (f32[512,64]{0,1:T(8,128)S(1)}, f32[512,64]{0,1:T(8,128)S(1)}, u32[]{:S(2)}, u32[]{:S(2)}) collective-permute-start(f32[512,64]{0,1:T(8,128)S(1)} %fusion.40), channel_id=1, source_target_pairs={{0,8},{8,0},{16,24},{24,16},{32,40},{40,32},{48,56},{56,48},{1,9},... | collective-permute-start | bytes 393224 | tf_op jit(solution)/shard_map/ppermute | solution.py:22
  195.8 7.8 %collective-permute-start.20 = (f32[512,64]{0,1:T(8,128)S(1)}, f32[512,64]{0,1:T(8,128)S(1)}, u32[]{:S(2)}, u32[]{:S(2)}) collective-permute-start(f32[512,64]{0,1:T(8,128)S(1)} %add.383), channel_id=1, source_target_pairs={{0,16},{8,24},{16,0},{24,8},{32,48},{40,56},{48,32},{56,40},{1,17}... | collective-permute-start | bytes 393224 | tf_op jit(solution)/shard_map/ppermute | solution.py:22
  199.2 8.3 %collective-permute-start.15 = (f32[2]{0:T(128)S(1)}, f32[2]{0:T(128)S(1)}, u32[]{:S(2)}, u32[]{:S(2)}) collective-permute-start(f32[2]{0:T(128)S(1)} %fusion.127), channel_id=1, source_target_pairs={{0,8},{8,0},{16,24},{24,16},{32,40},{40,32},{48,56},{56,48},{1,9},... | collective-permute-start | bytes 32 | tf_op jit(solution)/shard_map/ppermute | solution.py:22
  203.6 21.5 %collective-permute-start.21 = (f32[512,64]{0,1:T(8,128)S(1)}, f32[512,64]{0,1:T(8,128)S(1)}, u32[]{:S(2)}, u32[]{:S(2)}) collective-permute-start(f32[512,64]{0,1:T(8,128)S(1)} %add.384), channel_id=1, source_target_pairs={{0,32},{8,40},{16,48},{24,56},{32,0},{40,8},{48,16},{56,24},{1,33}... | collective-permute-start | bytes 393224 | tf_op jit(solution)/shard_map/ppermute | solution.py:22
  208.9 6.3 %collective-permute-start.16 = (f32[2]{0:T(128)S(1)}, f32[2]{0:T(128)S(1)}, u32[]{:S(2)}, u32[]{:S(2)}) collective-permute-start(f32[2]{0:T(128)S(1)} %fusion.133), channel_id=1, source_target_pairs={{0,16},{8,24},{16,0},{24,8},{32,48},{40,56},{48,32},{56,40},{1,17}... | collective-permute-start | bytes 32 | tf_op jit(solution)/shard_map/ppermute | solution.py:22
  215.2 9.3 %collective-permute-start.17 = (f32[2]{0:T(128)S(1)}, f32[2]{0:T(128)S(1)}, u32[]{:S(2)}, u32[]{:S(2)}) collective-permute-start(f32[2]{0:T(128)S(1)} %add.380), channel_id=1, source_target_pairs={{0,32},{8,40},{16,48},{24,56},{32,0},{40,8},{48,16},{56,24},{1,33}... | collective-permute-start | bytes 32 | tf_op jit(solution)/shard_map/ppermute | solution.py:22
  238.0 6.9 %collective-permute-start.24 = (f32[2]{0:T(128)S(1)}, f32[2]{0:T(128)S(1)}, u32[]{:S(2)}, u32[]{:S(2)}) collective-permute-start(f32[2]{0:T(128)S(1)} %fusion.132), channel_id=1, source_target_pairs={{0,4},{2,6},{4,0},{6,2},{1,5},{3,7},{5,1},{7,3},{8,12},{10,14},{12... | collective-permute-start | bytes 32 | tf_op jit(solution)/shard_map/ppermute | solution.py:22
  244.9 6.3 %collective-permute-start.25 = (f32[2]{0:T(128)S(1)}, f32[2]{0:T(128)S(1)}, u32[]{:S(2)}, u32[]{:S(2)}) collective-permute-start(f32[2]{0:T(128)S(1)} %add.390), channel_id=1, source_target_pairs={{0,128},{128,0},{256,384},{384,256},{1,129},{129,1},{257,385},{385... | collective-permute-start | bytes 32 | tf_op jit(solution)/shard_map/ppermute | solution.py:22
  251.2 9.3 %collective-permute-start.26 = (f32[2]{0:T(128)S(1)}, f32[2]{0:T(128)S(1)}, u32[]{:S(2)}, u32[]{:S(2)}) collective-permute-start(f32[2]{0:T(128)S(1)} %add.391), channel_id=1, source_target_pairs={{0,256},{128,384},{256,0},{384,128},{1,257},{129,385},{257,1},{385... | collective-permute-start | bytes 32 | tf_op jit(solution)/shard_map/ppermute | solution.py:22
  266.0 6.9 %collective-permute-start.32 = (f32[512,64]{0,1:T(8,128)S(1)}, f32[512,64]{0,1:T(8,128)S(1)}, u32[]{:S(2)}, u32[]{:S(2)}) collective-permute-start(f32[512,64]{0,1:T(8,128)S(1)} %pad_maximum_fusion.3), channel_id=1, source_target_pairs={{0,64},{64,0},{1,65},{65,1},{2,66},{66,2},{3,67},{67,3},{4,68},{68... | collective-permute-start | bytes 393224 | tf_op jit(solution)/shard_map/ppermute | solution.py:22
  269.6 6.7 %collective-permute-start.27 = (f32[256,32]{0,1:T(8,128)S(1)}, f32[256,32]{0,1:T(8,128)S(1)}, u32[]{:S(2)}, u32[]{:S(2)}) collective-permute-start(f32[256,32]{0,1:T(8,128)S(1)} %convolution_add_fusion.4), channel_id=1, source_target_pairs={{0,1},{1,0},{2,3},{3,2},{4,5},{5,4},{6,7},{7,6},{8,9},{9,8},{10,11... | collective-permute-start | bytes 98312 | tf_op jit(solution)/shard_map/ppermute | solution.py:22
  272.9 27.5 %collective-permute-start.33 = (f32[512,64]{0,1:T(8,128)S(1)}, f32[512,64]{0,1:T(8,128)S(1)}, u32[]{:S(2)}, u32[]{:S(2)}) collective-permute-start(f32[512,64]{0,1:T(8,128)S(1)} %fusion.39), channel_id=1, source_target_pairs={{0,8},{8,0},{16,24},{24,16},{32,40},{40,32},{48,56},{56,48},{1,9},... | collective-permute-start | bytes 393224 | tf_op jit(solution)/shard_map/ppermute | solution.py:22
  282.1 7.3 %collective-permute-start.29 = (f32[256,32]{0,1:T(8,128)S(1)}, f32[256,32]{0,1:T(8,128)S(1)}, u32[]{:S(2)}, u32[]{:S(2)}) collective-permute-start(f32[256,32]{0,1:T(8,128)S(1)} %add.400), channel_id=1, source_target_pairs={{0,4},{2,6},{4,0},{6,2},{1,5},{3,7},{5,1},{7,3},{8,12},{10,14},{12... | collective-permute-start | bytes 98312 | tf_op jit(solution)/shard_map/ppermute | solution.py:22
  289.4 6.9 %collective-permute-start.30 = (f32[256,32]{0,1:T(8,128)S(1)}, f32[256,32]{0,1:T(8,128)S(1)}, u32[]{:S(2)}, u32[]{:S(2)}) collective-permute-start(f32[256,32]{0,1:T(8,128)S(1)} %add.401), channel_id=1, source_target_pairs={{0,128},{128,0},{256,384},{384,256},{1,129},{129,1},{257,385},{385... | collective-permute-start | bytes 98312 | tf_op jit(solution)/shard_map/ppermute | solution.py:22
  296.3 9.7 %collective-permute-start.31 = (f32[256,32]{0,1:T(8,128)S(1)}, f32[256,32]{0,1:T(8,128)S(1)}, u32[]{:S(2)}, u32[]{:S(2)}) collective-permute-start(f32[256,32]{0,1:T(8,128)S(1)} %add.402), channel_id=1, source_target_pairs={{0,256},{128,384},{256,0},{384,128},{1,257},{129,385},{257,1},{385... | collective-permute-start | bytes 98312 | tf_op jit(solution)/shard_map/ppermute | solution.py:22
  300.5 8.4 %collective-permute-start.34 = (f32[512,64]{0,1:T(8,128)S(1)}, f32[512,64]{0,1:T(8,128)S(1)}, u32[]{:S(2)}, u32[]{:S(2)}) collective-permute-start(f32[512,64]{0,1:T(8,128)S(1)} %add.405), channel_id=1, source_target_pairs={{0,16},{8,24},{16,0},{24,8},{32,48},{40,56},{48,32},{56,40},{1,17}... | collective-permute-start | bytes 393224 | tf_op jit(solution)/shard_map/ppermute | solution.py:22
  308.9 13.6 %collective-permute-start.35 = (f32[512,64]{0,1:T(8,128)S(1)}, f32[512,64]{0,1:T(8,128)S(1)}, u32[]{:S(2)}, u32[]{:S(2)}) collective-permute-start(f32[512,64]{0,1:T(8,128)S(1)} %add.406), channel_id=1, source_target_pairs={{0,32},{8,40},{16,48},{24,56},{32,0},{40,8},{48,16},{56,24},{1,33}... | collective-permute-start | bytes 393224 | tf_op jit(solution)/shard_map/ppermute | solution.py:22
  327.8 27.4 %collective-permute-start.45 = (f32[512,64]{0,1:T(8,128)S(1)}, f32[512,64]{0,1:T(8,128)S(1)}, u32[]{:S(2)}, u32[]{:S(2)}) collective-permute-start(f32[512,64]{0,1:T(8,128)S(1)} %pad_maximum_fusion.4), channel_id=1, source_target_pairs={{0,64},{64,0},{1,65},{65,1},{2,66},{66,2},{3,67},{67,3},{4,68},{68... | collective-permute-start | bytes 393224 | tf_op jit(solution)/shard_map/ppermute | solution.py:22
  335.5 7.3 %collective-permute-start.38 = (f32[256,32]{0,1:T(8,128)S(1)}, f32[256,32]{0,1:T(8,128)S(1)}, u32[]{:S(2)}, u32[]{:S(2)}) collective-permute-start(f32[256,32]{0,1:T(8,128)S(1)} %add.411), channel_id=1, source_target_pairs={{0,4},{2,6},{4,0},{6,2},{1,5},{3,7},{5,1},{7,3},{8,12},{10,14},{12... | collective-permute-start | bytes 98312 | tf_op jit(solution)/shard_map/ppermute | solution.py:22
  342.8 6.7 %collective-permute-start.39 = (f32[256,32]{0,1:T(8,128)S(1)}, f32[256,32]{0,1:T(8,128)S(1)}, u32[]{:S(2)}, u32[]{:S(2)}) collective-permute-start(f32[256,32]{0,1:T(8,128)S(1)} %add.412), channel_id=1, source_target_pairs={{0,128},{128,0},{256,384},{384,256},{1,129},{129,1},{257,385},{385... | collective-permute-start | bytes 98312 | tf_op jit(solution)/shard_map/ppermute | solution.py:22
  349.6 9.7 %collective-permute-start.40 = (f32[256,32]{0,1:T(8,128)S(1)}, f32[256,32]{0,1:T(8,128)S(1)}, u32[]{:S(2)}, u32[]{:S(2)}) collective-permute-start(f32[256,32]{0,1:T(8,128)S(1)} %add.413), channel_id=1, source_target_pairs={{0,256},{128,384},{256,0},{384,128},{1,257},{129,385},{257,1},{385... | collective-permute-start | bytes 98312 | tf_op jit(solution)/shard_map/ppermute | solution.py:22
  355.2 10.9 %collective-permute-start.46 = (f32[512,64]{0,1:T(8,128)S(1)}, f32[512,64]{0,1:T(8,128)S(1)}, u32[]{:S(2)}, u32[]{:S(2)}) collective-permute-start(f32[512,64]{0,1:T(8,128)S(1)} %fusion.38), channel_id=1, source_target_pairs={{0,8},{8,0},{16,24},{24,16},{32,40},{40,32},{48,56},{56,48},{1,9},... | collective-permute-start | bytes 393224 | tf_op jit(solution)/shard_map/ppermute | solution.py:22
  361.9 6.1 %collective-permute-start.41 = (f32[2]{0:T(128)S(1)}, f32[2]{0:T(128)S(1)}, u32[]{:S(2)}, u32[]{:S(2)}) collective-permute-start(f32[2]{0:T(128)S(1)} %pad_maximum_fusion.9), channel_id=1, source_target_pairs={{0,64},{64,0},{1,65},{65,1},{2,66},{66,2},{3,67},{67,3},{4,68},{68... | collective-permute-start | bytes 32 | tf_op jit(solution)/shard_map/ppermute | solution.py:22
  366.1 8.3 %collective-permute-start.47 = (f32[512,64]{0,1:T(8,128)S(1)}, f32[512,64]{0,1:T(8,128)S(1)}, u32[]{:S(2)}, u32[]{:S(2)}) collective-permute-start(f32[512,64]{0,1:T(8,128)S(1)} %add.421), channel_id=1, source_target_pairs={{0,16},{8,24},{16,0},{24,8},{32,48},{40,56},{48,32},{56,40},{1,17}... | collective-permute-start | bytes 393224 | tf_op jit(solution)/shard_map/ppermute | solution.py:22
  369.5 14.2 %collective-permute-start.42 = (f32[2]{0:T(128)S(1)}, f32[2]{0:T(128)S(1)}, u32[]{:S(2)}, u32[]{:S(2)}) collective-permute-start(f32[2]{0:T(128)S(1)} %fusion.125), channel_id=1, source_target_pairs={{0,8},{8,0},{16,24},{24,16},{32,40},{40,32},{48,56},{56,48},{1,9},... | collective-permute-start | bytes 32 | tf_op jit(solution)/shard_map/ppermute | solution.py:22
  374.5 26.9 %collective-permute-start.48 = (f32[512,64]{0,1:T(8,128)S(1)}, f32[512,64]{0,1:T(8,128)S(1)}, u32[]{:S(2)}, u32[]{:S(2)}) collective-permute-start(f32[512,64]{0,1:T(8,128)S(1)} %add.422), channel_id=1, source_target_pairs={{0,32},{8,40},{16,48},{24,56},{32,0},{40,8},{48,16},{56,24},{1,33}... | collective-permute-start | bytes 393224 | tf_op jit(solution)/shard_map/ppermute | solution.py:22
  385.1 6.3 %collective-permute-start.43 = (f32[2]{0:T(128)S(1)}, f32[2]{0:T(128)S(1)}, u32[]{:S(2)}, u32[]{:S(2)}) collective-permute-start(f32[2]{0:T(128)S(1)} %fusion.131), channel_id=1, source_target_pairs={{0,16},{8,24},{16,0},{24,8},{32,48},{40,56},{48,32},{56,40},{1,17}... | collective-permute-start | bytes 32 | tf_op jit(solution)/shard_map/ppermute | solution.py:22
  391.4 9.3 %collective-permute-start.44 = (f32[2]{0:T(128)S(1)}, f32[2]{0:T(128)S(1)}, u32[]{:S(2)}, u32[]{:S(2)}) collective-permute-start(f32[2]{0:T(128)S(1)} %add.418), channel_id=1, source_target_pairs={{0,32},{8,40},{16,48},{24,56},{32,0},{40,8},{48,16},{56,24},{1,33}... | collective-permute-start | bytes 32 | tf_op jit(solution)/shard_map/ppermute | solution.py:22
  414.2 6.9 %collective-permute-start.51 = (f32[2]{0:T(128)S(1)}, f32[2]{0:T(128)S(1)}, u32[]{:S(2)}, u32[]{:S(2)}) collective-permute-start(f32[2]{0:T(128)S(1)} %fusion.130), channel_id=1, source_target_pairs={{0,4},{2,6},{4,0},{6,2},{1,5},{3,7},{5,1},{7,3},{8,12},{10,14},{12... | collective-permute-start | bytes 32 | tf_op jit(solution)/shard_map/ppermute | solution.py:22
  421.2 6.3 %collective-permute-start.52 = (f32[2]{0:T(128)S(1)}, f32[2]{0:T(128)S(1)}, u32[]{:S(2)}, u32[]{:S(2)}) collective-permute-start(f32[2]{0:T(128)S(1)} %add.428), channel_id=1, source_target_pairs={{0,128},{128,0},{256,384},{384,256},{1,129},{129,1},{257,385},{385... | collective-permute-start | bytes 32 | tf_op jit(solution)/shard_map/ppermute | solution.py:22
  427.5 9.3 %collective-permute-start.53 = (f32[2]{0:T(128)S(1)}, f32[2]{0:T(128)S(1)}, u32[]{:S(2)}, u32[]{:S(2)}) collective-permute-start(f32[2]{0:T(128)S(1)} %add.429), channel_id=1, source_target_pairs={{0,256},{128,384},{256,0},{384,128},{1,257},{129,385},{257,1},{385... | collective-permute-start | bytes 32 | tf_op jit(solution)/shard_map/ppermute | solution.py:22
  442.3 6.9 %collective-permute-start.59 = (f32[512,64]{0,1:T(8,128)S(1)}, f32[512,64]{0,1:T(8,128)S(1)}, u32[]{:S(2)}, u32[]{:S(2)}) collective-permute-start(f32[512,64]{0,1:T(8,128)S(1)} %pad_maximum_fusion.5), channel_id=1, source_target_pairs={{0,64},{64,0},{1,65},{65,1},{2,66},{66,2},{3,67},{67,3},{4,68},{68... | collective-permute-start | bytes 393224 | tf_op jit(solution)/shard_map/ppermute | solution.py:22
  449.2 26.7 %collective-permute-start.60 = (f32[512,64]{0,1:T(8,128)S(1)}, f32[512,64]{0,1:T(8,128)S(1)}, u32[]{:S(2)}, u32[]{:S(2)}) collective-permute-start(f32[512,64]{0,1:T(8,128)S(1)} %fusion.37), channel_id=1, source_target_pairs={{0,8},{8,0},{16,24},{24,16},{32,40},{40,32},{48,56},{56,48},{1,9},... | collective-permute-start | bytes 393224 | tf_op jit(solution)/shard_map/ppermute | solution.py:22
  456.9 7.3 %collective-permute-start.56 = (f32[256,32]{0,1:T(8,128)S(1)}, f32[256,32]{0,1:T(8,128)S(1)}, u32[]{:S(2)}, u32[]{:S(2)}) collective-permute-start(f32[256,32]{0,1:T(8,128)S(1)} %add.438), channel_id=1, source_target_pairs={{0,4},{2,6},{4,0},{6,2},{1,5},{3,7},{5,1},{7,3},{8,12},{10,14},{12... | collective-permute-start | bytes 98312 | tf_op jit(solution)/shard_map/ppermute | solution.py:22
  464.2 6.7 %collective-permute-start.57 = (f32[256,32]{0,1:T(8,128)S(1)}, f32[256,32]{0,1:T(8,128)S(1)}, u32[]{:S(2)}, u32[]{:S(2)}) collective-permute-start(f32[256,32]{0,1:T(8,128)S(1)} %add.439), channel_id=1, source_target_pairs={{0,128},{128,0},{256,384},{384,256},{1,129},{129,1},{257,385},{385... | collective-permute-start | bytes 98312 | tf_op jit(solution)/shard_map/ppermute | solution.py:22
  470.9 10.1 %collective-permute-start.58 = (f32[256,32]{0,1:T(8,128)S(1)}, f32[256,32]{0,1:T(8,128)S(1)}, u32[]{:S(2)}, u32[]{:S(2)}) collective-permute-start(f32[256,32]{0,1:T(8,128)S(1)} %add.440), channel_id=1, source_target_pairs={{0,256},{128,384},{256,0},{384,128},{1,257},{129,385},{257,1},{385... | collective-permute-start | bytes 98312 | tf_op jit(solution)/shard_map/ppermute | solution.py:22
  475.9 10.6 %collective-permute-start.61 = (f32[512,64]{0,1:T(8,128)S(1)}, f32[512,64]{0,1:T(8,128)S(1)}, u32[]{:S(2)}, u32[]{:S(2)}) collective-permute-start(f32[512,64]{0,1:T(8,128)S(1)} %add.443), channel_id=1, source_target_pairs={{0,16},{8,24},{16,0},{24,8},{32,48},{40,56},{48,32},{56,40},{1,17}... | collective-permute-start | bytes 393224 | tf_op jit(solution)/shard_map/ppermute | solution.py:22
  486.5 10.8 %collective-permute-start.62 = (f32[512,64]{0,1:T(8,128)S(1)}, f32[512,64]{0,1:T(8,128)S(1)}, u32[]{:S(2)}, u32[]{:S(2)}) collective-permute-start(f32[512,64]{0,1:T(8,128)S(1)} %add.444), channel_id=1, source_target_pairs={{0,32},{8,40},{16,48},{24,56},{32,0},{40,8},{48,16},{56,24},{1,33}... | collective-permute-start | bytes 393224 | tf_op jit(solution)/shard_map/ppermute | solution.py:22
  502.7 26.0 %collective-permute-start.72 = (f32[512,64]{0,1:T(8,128)S(1)}, f32[512,64]{0,1:T(8,128)S(1)}, u32[]{:S(2)}, u32[]{:S(2)}) collective-permute-start(f32[512,64]{0,1:T(8,128)S(1)} %pad_maximum_fusion.6), channel_id=1, source_target_pairs={{0,64},{64,0},{1,65},{65,1},{2,66},{66,2},{3,67},{67,3},{4,68},{68... | collective-permute-start | bytes 393224 | tf_op jit(solution)/shard_map/ppermute | solution.py:22
  510.4 7.3 %collective-permute-start.65 = (f32[256,32]{0,1:T(8,128)S(1)}, f32[256,32]{0,1:T(8,128)S(1)}, u32[]{:S(2)}, u32[]{:S(2)}) collective-permute-start(f32[256,32]{0,1:T(8,128)S(1)} %add.449), channel_id=1, source_target_pairs={{0,4},{2,6},{4,0},{6,2},{1,5},{3,7},{5,1},{7,3},{8,12},{10,14},{12... | collective-permute-start | bytes 98312 | tf_op jit(solution)/shard_map/ppermute | solution.py:22
  517.7 6.7 %collective-permute-start.66 = (f32[256,32]{0,1:T(8,128)S(1)}, f32[256,32]{0,1:T(8,128)S(1)}, u32[]{:S(2)}, u32[]{:S(2)}) collective-permute-start(f32[256,32]{0,1:T(8,128)S(1)} %add.450), channel_id=1, source_target_pairs={{0,128},{128,0},{256,384},{384,256},{1,129},{129,1},{257,385},{385... | collective-permute-start | bytes 98312 | tf_op jit(solution)/shard_map/ppermute | solution.py:22
  524.4 9.7 %collective-permute-start.67 = (f32[256,32]{0,1:T(8,128)S(1)}, f32[256,32]{0,1:T(8,128)S(1)}, u32[]{:S(2)}, u32[]{:S(2)}) collective-permute-start(f32[256,32]{0,1:T(8,128)S(1)} %add.451), channel_id=1, source_target_pairs={{0,256},{128,384},{256,0},{384,128},{1,257},{129,385},{257,1},{385... | collective-permute-start | bytes 98312 | tf_op jit(solution)/shard_map/ppermute | solution.py:22
  528.7 12.0 %collective-permute-start.73 = (f32[512,64]{0,1:T(8,128)S(1)}, f32[512,64]{0,1:T(8,128)S(1)}, u32[]{:S(2)}, u32[]{:S(2)}) collective-permute-start(f32[512,64]{0,1:T(8,128)S(1)} %fusion.36), channel_id=1, source_target_pairs={{0,8},{8,0},{16,24},{24,16},{32,40},{40,32},{48,56},{56,48},{1,9},... | collective-permute-start | bytes 393224 | tf_op jit(solution)/shard_map/ppermute | solution.py:22
  536.9 6.8 %collective-permute-start.68 = (f32[2]{0:T(128)S(1)}, f32[2]{0:T(128)S(1)}, u32[]{:S(2)}, u32[]{:S(2)}) collective-permute-start(f32[2]{0:T(128)S(1)} %pad_maximum_fusion.11), channel_id=1, source_target_pairs={{0,64},{64,0},{1,65},{65,1},{2,66},{66,2},{3,67},{67,3},{4,68},{68... | collective-permute-start | bytes 32 | tf_op jit(solution)/shard_map/ppermute | solution.py:22
  540.8 10.1 %collective-permute-start.74 = (f32[512,64]{0,1:T(8,128)S(1)}, f32[512,64]{0,1:T(8,128)S(1)}, u32[]{:S(2)}, u32[]{:S(2)}) collective-permute-start(f32[512,64]{0,1:T(8,128)S(1)} %add.459), channel_id=1, source_target_pairs={{0,16},{8,24},{16,0},{24,8},{32,48},{40,56},{48,32},{56,40},{1,17}... | collective-permute-start | bytes 393224 | tf_op jit(solution)/shard_map/ppermute | solution.py:22
  545.1 7.8 %collective-permute-start.69 = (f32[2]{0:T(128)S(1)}, f32[2]{0:T(128)S(1)}, u32[]{:S(2)}, u32[]{:S(2)}) collective-permute-start(f32[2]{0:T(128)S(1)} %fusion.123), channel_id=1, source_target_pairs={{0,8},{8,0},{16,24},{24,16},{32,40},{40,32},{48,56},{56,48},{1,9},... | collective-permute-start | bytes 32 | tf_op jit(solution)/shard_map/ppermute | solution.py:22
  550.9 19.6 %collective-permute-start.75 = (f32[512,64]{0,1:T(8,128)S(1)}, f32[512,64]{0,1:T(8,128)S(1)}, u32[]{:S(2)}, u32[]{:S(2)}) collective-permute-start(f32[512,64]{0,1:T(8,128)S(1)} %add.460), channel_id=1, source_target_pairs={{0,32},{8,40},{16,48},{24,56},{32,0},{40,8},{48,16},{56,24},{1,33}... | collective-permute-start | bytes 393224 | tf_op jit(solution)/shard_map/ppermute | solution.py:22
  554.2 6.4 %collective-permute-start.70 = (f32[2]{0:T(128)S(1)}, f32[2]{0:T(128)S(1)}, u32[]{:S(2)}, u32[]{:S(2)}) collective-permute-start(f32[2]{0:T(128)S(1)} %fusion.129), channel_id=1, source_target_pairs={{0,16},{8,24},{16,0},{24,8},{32,48},{40,56},{48,32},{56,40},{1,17}... | collective-permute-start | bytes 32 | tf_op jit(solution)/shard_map/ppermute | solution.py:22
  560.6 9.3 %collective-permute-start.71 = (f32[2]{0:T(128)S(1)}, f32[2]{0:T(128)S(1)}, u32[]{:S(2)}, u32[]{:S(2)}) collective-permute-start(f32[2]{0:T(128)S(1)} %add.456), channel_id=1, source_target_pairs={{0,32},{8,40},{16,48},{24,56},{32,0},{40,8},{48,16},{56,24},{1,33}... | collective-permute-start | bytes 32 | tf_op jit(solution)/shard_map/ppermute | solution.py:22
  583.4 6.9 %collective-permute-start.78 = (f32[2]{0:T(128)S(1)}, f32[2]{0:T(128)S(1)}, u32[]{:S(2)}, u32[]{:S(2)}) collective-permute-start(f32[2]{0:T(128)S(1)} %fusion.128), channel_id=1, source_target_pairs={{0,4},{2,6},{4,0},{6,2},{1,5},{3,7},{5,1},{7,3},{8,12},{10,14},{12... | collective-permute-start | bytes 32 | tf_op jit(solution)/shard_map/ppermute | solution.py:22
  590.3 6.3 %collective-permute-start.79 = (f32[2]{0:T(128)S(1)}, f32[2]{0:T(128)S(1)}, u32[]{:S(2)}, u32[]{:S(2)}) collective-permute-start(f32[2]{0:T(128)S(1)} %add.466), channel_id=1, source_target_pairs={{0,128},{128,0},{256,384},{384,256},{1,129},{129,1},{257,385},{385... | collective-permute-start | bytes 32 | tf_op jit(solution)/shard_map/ppermute | solution.py:22
  596.6 9.3 %collective-permute-start.80 = (f32[2]{0:T(128)S(1)}, f32[2]{0:T(128)S(1)}, u32[]{:S(2)}, u32[]{:S(2)}) collective-permute-start(f32[2]{0:T(128)S(1)} %add.467), channel_id=1, source_target_pairs={{0,256},{128,384},{256,0},{384,128},{1,257},{129,385},{257,1},{385... | collective-permute-start | bytes 32 | tf_op jit(solution)/shard_map/ppermute | solution.py:22
  (20 other events, 141.9 us)
where the time goes:
time: 614 us; the launch traced here: 611 us
  starting transfers between devices  281 us (46%)
  waiting for transfers between devices  177 us (29%)
  blocking collectives  73.5 us (12%)
  other arithmetic  39.6 us (6%)
  matrix products  16.2 us (3%)
  local copies, waits for them, and re-layouts  13.5 us (2%)
  between operations  9.89 us (2%)
    ppermute x81, starting transfers between devices, doubling_sum(): value = value + lax.ppermute(value, name, pairs)  274 us
    ppermute x81, waiting for transfers between devices, doubling_sum(): value = value + lax.ppermute(value, name, pairs)  177 us
    all_gather x1, blocking collectives, per_device(): f_zero = lax.all_gather(freqs, ROW_GROUP, axis=0, tiled=True)  40.7 us
    all_gather x1, blocking collectives, per_device(): q_zero = lax.all_gather(q_own, 'yh', axis=0, tiled=True)  32.8 us
    add x75, other arithmetic, doubling_sum(): value = value + lax.ppermute(value, name, pairs)  16.6 us
  transfers between devices with their start and end apart: 82, of which 57 were waited for; matrix products, arithmetic and copies ran while one was open for 3% of the time, Pallas kernels for 0%

commit v1 on v0

--- a/solution.py
+++ b/solution.py
@@ -35,7 +35,8 @@
     own_snps = freqs.shape[0]
     q_own = ancestry / jnp.sum(ancestry, axis=1, keepdims=True)
     q_zero = lax.all_gather(q_own, "yh", axis=0, tiled=True)
-    f_zero = lax.all_gather(freqs, ROW_GROUP, axis=0, tiled=True)
+    sent = jnp.stack([freqs] * lax.axis_size(ROW_GROUP))
+    f_zero = jnp.concatenate(lax.all_to_all(sent, ROW_GROUP, 0, 0), axis=0)
 
     def em_map(q_rows, f_state):
         prob = jnp.dot(q_rows, f_state.T, precision=high, preferred_element_type=jnp.float32)

time: 614 us -> 594 us (0.967)
  blocking collectives: 73.5 us -> 31.9 us
  starting transfers between devices: 281 us -> 307 us
  waiting for transfers between devices: 177 us -> 169 us
    all_gather x1 -> x0, blocking collectives: 40.7 us -> none  [per_device(): f_zero = lax.all_gather(freqs, ROW_GROUP, axis=0, tiled=True)]
    ppermute x81, starting transfers between devices: 274 us -> 288 us  [doubling_sum(): value = value + lax.ppermute(value, name, pairs)]
    all_to_all x0 -> x1, starting transfers between devices: none -> 11.8 us  [per_device(): f_zero = jnp.concatenate(lax.all_to_all(sent, ROW_GROUP, 0, 0), axis=0)]
    ppermute x81, waiting for transfers between devices: 177 us -> 169 us  [doubling_sum(): value = value + lax.ppermute(value, name, pairs)]
  transfers between devices with their start and end apart: 82 -> 83, of which waited for: 57 -> 56; matrix products, arithmetic and copies ran while one was open for 3% -> 5% of each run, Pallas kernels for 0% -> 0%
where the time goes in v1:
time: 594 us; the launch traced here: 590 us
  starting transfers between devices  307 us (52%)
  waiting for transfers between devices  169 us (28%)
  other arithmetic  41.2 us (7%)
  blocking collectives  31.9 us (5%)
  matrix products  16.2 us (3%)
  local copies, waits for them, and re-layouts  14.5 us (2%)
  between operations  10.1 us (2%)
    ppermute x81, starting transfers between devices, doubling_sum(): value = value + lax.ppermute(value, name, pairs)  288 us
    ppermute x81, waiting for transfers between devices, doubling_sum(): value = value + lax.ppermute(value, name, pairs)  169 us
    all_gather x1, blocking collectives, per_device(): q_zero = lax.all_gather(q_own, 'yh', axis=0, tiled=True)  31.9 us
    add x75, other arithmetic, doubling_sum(): value = value + lax.ppermute(value, name, pairs)  17.1 us
  transfers between devices with their start and end apart: 83, of which 56 were waited for; matrix products, arithmetic and copies ran while one was open for 5% of the time, Pallas kernels for 0%

profile of v1, /device:TPU:56, one launch (start us, length us, event | category | flops | bytes accessed | tf_op | source)
XLA Modules:
  0.0 590.5 jit_solution(14750352266712451854)
XLA Ops:
  2.3 11.8 %all-to-all-start.1 = ((f32[16,1,1024]{2,1,0:T(1,128)}), f32[16,1,1024]{2,1,0:T(1,128)S(1)}, u32[]{:S(2)}, u32[]{:S(2)}) async-start(f32[16,1,1024]{2,1,0:T(1,128)} %reshape.56), calls=%async_computation.1 | async-start | bytes 131072 | tf_op jit(solution)/shard_map/all_to_all | solution.py:39
  21.5 7.0 %all-to-all-start = ((f32[4,1,65536]{2,1,0:T(1,128)}), f32[4,1,65536]{2,1,0:T(1,128)S(1)}, u32[]{:S(2)}, u32[]{:S(2)}) async-start(f32[4,1,65536]{2,1,0:T(1,128)} %reshape.58), calls=%async_computation | async-start | bytes 2097152 | tf_op jit(solution)/shard_map/all_to_all | solution.py:32
  28.5 31.9 %all-gather = f32[4,64,32]{1,2,0:T(8,128)S(1)} all-gather(f32[1,64,32]{1,2,0:T(8,128)S(1)} %divide_bitcast_fusion), channel_id=1, replica_groups=mesh['yh'=4,'yl'=2,'z'=8,'x'=4,'c'=2] {'yh'}, dimensions={0}, use_global_device_ids=true | all-gather | bytes 40960 | tf_op jit(solution)/shard_map/all_gather | solution.py:37
  62.3 3.7 reduce
  77.7 3.8 collective-permute-start.6
  81.6 3.4 collective-permute-start.1
  87.4 4.9 collective-permute-start.2
  97.2 4.2 collective-permute-done.3
  101.4 4.6 collective-permute-start.4
  106.1 4.3 collective-permute-start.7
  111.2 3.9 collective-permute-done.7
  115.1 9.2 %collective-permute-start.8 = (f32[512,64]{0,1:T(8,128)S(1)}, f32[512,64]{0,1:T(8,128)S(1)}, u32[]{:S(2)}, u32[]{:S(2)}) collective-permute-start(f32[512,64]{0,1:T(8,128)S(1)} %add.368), channel_id=1, source_target_pairs={{0,32},{8,40},{16,48},{24,56},{32,0},{40,8},{48,16},{56,24},{1,33}... | collective-permute-start | bytes 393224 | tf_op jit(solution)/shard_map/ppermute | solution.py:22
  134.6 3.4 collective-permute-start.10
  140.4 4.9 collective-permute-start.11
  150.8 3.6 collective-permute-done.12
  154.4 4.9 collective-permute-start.13
  166.1 3.7 collective-permute-start.14
  173.2 4.2 collective-permute-start.15
  177.9 9.3 %collective-permute-start.21 = (f32[512,64]{0,1:T(8,128)S(1)}, f32[512,64]{0,1:T(8,128)S(1)}, u32[]{:S(2)}, u32[]{:S(2)}) collective-permute-start(f32[512,64]{0,1:T(8,128)S(1)} %add.384), channel_id=1, source_target_pairs={{0,32},{8,40},{16,48},{24,56},{32,0},{40,8},{48,16},{56,24},{1,33}... | collective-permute-start | bytes 393224 | tf_op jit(solution)/shard_map/ppermute | solution.py:22
  190.5 4.4 collective-permute-done.16
  196.9 7.4 %collective-permute-done.17 = f32[2]{0:T(128)S(1)} collective-permute-done((f32[2]{0:T(128)S(1)}, f32[2]{0:T(128)S(1)}, u32[]{:S(2)}, u32[]{:S(2)}) %collective-permute-start.17) | collective-permute-done | bytes 40 | tf_op jit(solution)/shard_map/ppermute | solution.py:22
  211.4 3.4 collective-permute-start.23
  218.2 4.9 collective-permute-start.24
  231.5 5.2 collective-permute-start.26
  236.6 4.2 collective-permute-done.26
  255.1 3.4 collective-permute-start.28
  261.0 4.9 collective-permute-start.29
  275.0 5.2 collective-permute-start.31
  280.2 4.5 collective-permute-start.34
  284.7 5.5 collective-permute-done.34
  292.2 8.8 %collective-permute-done.35 = f32[512,64]{0,1:T(8,128)S(1)} collective-permute-done((f32[512,64]{0,1:T(8,128)S(1)}, f32[512,64]{0,1:T(8,128)S(1)}, u32[]{:S(2)}, u32[]{:S(2)}) %collective-permute-start.35) | collective-permute-done | bytes 131104 | tf_op jit(solution)/shard_map/ppermute | solution.py:22
  308.3 3.4 collective-permute-start.37
  314.1 4.9 collective-permute-start.38
  323.9 4.1 collective-permute-done.39
  328.1 4.6 collective-permute-start.40
  332.7 3.4 collective-permute-start.46
  340.4 4.3 collective-permute-start.41
  348.4 3.4 collective-permute-start.42
  359.9 4.4 collective-permute-done.43
  364.3 7.8 %collective-permute-start.44 = (f32[2]{0:T(128)S(1)}, f32[2]{0:T(128)S(1)}, u32[]{:S(2)}, u32[]{:S(2)}) collective-permute-start(f32[2]{0:T(128)S(1)} %add.418), channel_id=1, source_target_pairs={{0,32},{8,40},{16,48},{24,56},{32,0},{40,8},{48,16},{56,24},{1,33}... | collective-permute-start | bytes 32 | tf_op jit(solution)/shard_map/ppermute | solution.py:22
  387.5 4.9 collective-permute-start.51
  396.9 3.9 collective-permute-done.52
  400.8 4.2 collective-permute-start.53
  405.0 5.1 collective-permute-done.53
  424.5 3.4 collective-permute-start.55
  430.3 4.9 collective-permute-start.56
  440.0 4.6 collective-permute-done.57
  444.6 4.2 collective-permute-start.58
  448.9 4.3 collective-permute-start.61
  456.7 10.7 %collective-permute-start.62 = (f32[512,64]{0,1:T(8,128)S(1)}, f32[512,64]{0,1:T(8,128)S(1)}, u32[]{:S(2)}, u32[]{:S(2)}) collective-permute-start(f32[512,64]{0,1:T(8,128)S(1)} %add.444), channel_id=1, source_target_pairs={{0,32},{8,40},{16,48},{24,56},{32,0},{40,8},{48,16},{56,24},{1,33}... | collective-permute-start | bytes 393224 | tf_op jit(solution)/shard_map/ppermute | solution.py:22
  477.6 3.4 collective-permute-start.64
  483.4 4.9 collective-permute-start.65
  492.7 4.8 collective-permute-done.66
  497.4 4.8 collective-permute-start.67
  502.3 3.7 collective-permute-start.73
  510.1 3.6 collective-permute-start.68
  522.9 9.2 %collective-permute-start.75 = (f32[512,64]{0,1:T(8,128)S(1)}, f32[512,64]{0,1:T(8,128)S(1)}, u32[]{:S(2)}, u32[]{:S(2)}) collective-permute-start(f32[512,64]{0,1:T(8,128)S(1)} %add.460), channel_id=1, source_target_pairs={{0,32},{8,40},{16,48},{24,56},{32,0},{40,8},{48,16},{56,24},{1,33}... | collective-permute-start | bytes 393224 | tf_op jit(solution)/shard_map/ppermute | solution.py:22
  535.4 4.4 collective-permute-done.70
  541.7 7.4 %collective-permute-done.71 = f32[2]{0:T(128)S(1)} collective-permute-done((f32[2]{0:T(128)S(1)}, f32[2]{0:T(128)S(1)}, u32[]{:S(2)}, u32[]{:S(2)}) %collective-permute-start.71) | collective-permute-done | bytes 40 | tf_op jit(solution)/shard_map/ppermute | solution.py:22
  556.2 3.4 collective-permute-start.77
  563.0 4.9 collective-permute-start.78
  571.9 4.4 collective-permute-done.79
  576.3 4.8 collective-permute-start.80
  581.1 4.5 collective-permute-done.80
  (278 shorter events, 233.1 us)
Async XLA Ops:
  2.3 19.2 %all-to-all-start.1 = ((f32[16,1,1024]{2,1,0:T(1,128)}), f32[16,1,1024]{2,1,0:T(1,128)S(1)}, u32[]{:S(2)}, u32[]{:S(2)}) async-start(f32[16,1,1024]{2,1,0:T(1,128)} %reshape.56), calls=%async_computation.1 | async-start | bytes 131072 | tf_op jit(solution)/shard_map/all_to_all | solution.py:39
  21.5 40.8 %all-to-all-start = ((f32[4,1,65536]{2,1,0:T(1,128)}), f32[4,1,65536]{2,1,0:T(1,128)S(1)}, u32[]{:S(2)}, u32[]{:S(2)}) async-start(f32[4,1,65536]{2,1,0:T(1,128)} %reshape.58), calls=%async_computation | async-start | bytes 2097152 | tf_op jit(solution)/shard_map/all_to_all | solution.py:32
  70.9 6.9 %collective-permute-start.5 = (f32[512,64]{0,1:T(8,128)S(1)}, f32[512,64]{0,1:T(8,128)S(1)}, u32[]{:S(2)}, u32[]{:S(2)}) collective-permute-start(f32[512,64]{0,1:T(8,128)S(1)} %pad_maximum_fusion.1), channel_id=1, source_target_pairs={{0,64},{64,0},{1,65},{65,1},{2,66},{66,2},{3,67},{67,3},{4,68},{68... | collective-permute-start | bytes 393224 | tf_op jit(solution)/shard_map/ppermute | solution.py:22
  73.4 8.2 %collective-permute-start = (f32[256,32]{0,1:T(8,128)S(1)}, f32[256,32]{0,1:T(8,128)S(1)}, u32[]{:S(2)}, u32[]{:S(2)}) collective-permute-start(f32[256,32]{0,1:T(8,128)S(1)} %convolution_add_fusion.5), channel_id=1, source_target_pairs={{0,1},{1,0},{2,3},{3,2},{4,5},{5,4},{6,7},{7,6},{8,9},{9,8},{10,11... | collective-permute-start | bytes 98312 | tf_op jit(solution)/shard_map/ppermute | solution.py:22
  77.7 28.3 %collective-permute-start.6 = (f32[512,64]{0,1:T(8,128)S(1)}, f32[512,64]{0,1:T(8,128)S(1)}, u32[]{:S(2)}, u32[]{:S(2)}) collective-permute-start(f32[512,64]{0,1:T(8,128)S(1)} %fusion.40), channel_id=1, source_target_pairs={{0,8},{8,0},{16,24},{24,16},{32,40},{40,32},{48,56},{56,48},{1,9},... | collective-permute-start | bytes 393224 | tf_op jit(solution)/shard_map/ppermute | solution.py:22
  87.4 7.3 %collective-permute-start.2 = (f32[256,32]{0,1:T(8,128)S(1)}, f32[256,32]{0,1:T(8,128)S(1)}, u32[]{:S(2)}, u32[]{:S(2)}) collective-permute-start(f32[256,32]{0,1:T(8,128)S(1)} %add.362), channel_id=1, source_target_pairs={{0,4},{2,6},{4,0},{6,2},{1,5},{3,7},{5,1},{7,3},{8,12},{10,14},{12... | collective-permute-start | bytes 98312 | tf_op jit(solution)/shard_map/ppermute | solution.py:22
  94.7 6.7 %collective-permute-start.3 = (f32[256,32]{0,1:T(8,128)S(1)}, f32[256,32]{0,1:T(8,128)S(1)}, u32[]{:S(2)}, u32[]{:S(2)}) collective-permute-start(f32[256,32]{0,1:T(8,128)S(1)} %add.363), channel_id=1, source_target_pairs={{0,128},{128,0},{256,384},{384,256},{1,129},{129,1},{257,385},{385... | collective-permute-start | bytes 98312 | tf_op jit(solution)/shard_map/ppermute | solution.py:22
  101.4 9.7 %collective-permute-start.4 = (f32[256,32]{0,1:T(8,128)S(1)}, f32[256,32]{0,1:T(8,128)S(1)}, u32[]{:S(2)}, u32[]{:S(2)}) collective-permute-start(f32[256,32]{0,1:T(8,128)S(1)} %add.364), channel_id=1, source_target_pairs={{0,256},{128,384},{256,0},{384,128},{1,257},{129,385},{257,1},{385... | collective-permute-start | bytes 98312 | tf_op jit(solution)/shard_map/ppermute | solution.py:22
  106.1 9.0 %collective-permute-start.7 = (f32[512,64]{0,1:T(8,128)S(1)}, f32[512,64]{0,1:T(8,128)S(1)}, u32[]{:S(2)}, u32[]{:S(2)}) collective-permute-start(f32[512,64]{0,1:T(8,128)S(1)} %add.367), channel_id=1, source_target_pairs={{0,16},{8,24},{16,0},{24,8},{32,48},{40,56},{48,32},{56,40},{1,17}... | collective-permute-start | bytes 393224 | tf_op jit(solution)/shard_map/ppermute | solution.py:22
  115.1 12.0 %collective-permute-start.8 = (f32[512,64]{0,1:T(8,128)S(1)}, f32[512,64]{0,1:T(8,128)S(1)}, u32[]{:S(2)}, u32[]{:S(2)}) collective-permute-start(f32[512,64]{0,1:T(8,128)S(1)} %add.368), channel_id=1, source_target_pairs={{0,32},{8,40},{16,48},{24,56},{32,0},{40,8},{48,16},{56,24},{1,33}... | collective-permute-start | bytes 393224 | tf_op jit(solution)/shard_map/ppermute | solution.py:22
  132.4 26.9 %collective-permute-start.18 = (f32[512,64]{0,1:T(8,128)S(1)}, f32[512,64]{0,1:T(8,128)S(1)}, u32[]{:S(2)}, u32[]{:S(2)}) collective-permute-start(f32[512,64]{0,1:T(8,128)S(1)} %pad_maximum_fusion.2), channel_id=1, source_target_pairs={{0,64},{64,0},{1,65},{65,1},{2,66},{66,2},{3,67},{67,3},{4,68},{68... | collective-permute-start | bytes 393224 | tf_op jit(solution)/shard_map/ppermute | solution.py:22
  140.4 7.3 %collective-permute-start.11 = (f32[256,32]{0,1:T(8,128)S(1)}, f32[256,32]{0,1:T(8,128)S(1)}, u32[]{:S(2)}, u32[]{:S(2)}) collective-permute-start(f32[256,32]{0,1:T(8,128)S(1)} %add.373), channel_id=1, source_target_pairs={{0,4},{2,6},{4,0},{6,2},{1,5},{3,7},{5,1},{7,3},{8,12},{10,14},{12... | collective-permute-start | bytes 98312 | tf_op jit(solution)/shard_map/ppermute | solution.py:22
  147.7 6.7 %collective-permute-start.12 = (f32[256,32]{0,1:T(8,128)S(1)}, f32[256,32]{0,1:T(8,128)S(1)}, u32[]{:S(2)}, u32[]{:S(2)}) collective-permute-start(f32[256,32]{0,1:T(8,128)S(1)} %add.374), channel_id=1, source_target_pairs={{0,128},{128,0},{256,384},{384,256},{1,129},{129,1},{257,385},{385... | collective-permute-start | bytes 98312 | tf_op jit(solution)/shard_map/ppermute | solution.py:22
  154.4 9.7 %collective-permute-start.13 = (f32[256,32]{0,1:T(8,128)S(1)}, f32[256,32]{0,1:T(8,128)S(1)}, u32[]{:S(2)}, u32[]{:S(2)}) collective-permute-start(f32[256,32]{0,1:T(8,128)S(1)} %add.375), channel_id=1, source_target_pairs={{0,256},{128,384},{256,0},{384,128},{1,257},{129,385},{257,1},{385... | collective-permute-start | bytes 98312 | tf_op jit(solution)/shard_map/ppermute | solution.py:22
  159.4 10.4 %collective-permute-start.19 = (f32[512,64]{0,1:T(8,128)S(1)}, f32[512,64]{0,1:T(8,128)S(1)}, u32[]{:S(2)}, u32[]{:S(2)}) collective-permute-start(f32[512,64]{0,1:T(8,128)S(1)} %fusion.39), channel_id=1, source_target_pairs={{0,8},{8,0},{16,24},{24,16},{32,40},{40,32},{48,56},{56,48},{1,9},... | collective-permute-start | bytes 393224 | tf_op jit(solution)/shard_map/ppermute | solution.py:22
  169.8 8.1 %collective-permute-start.20 = (f32[512,64]{0,1:T(8,128)S(1)}, f32[512,64]{0,1:T(8,128)S(1)}, u32[]{:S(2)}, u32[]{:S(2)}) collective-permute-start(f32[512,64]{0,1:T(8,128)S(1)} %add.383), channel_id=1, source_target_pairs={{0,16},{8,24},{16,0},{24,8},{32,48},{40,56},{48,32},{56,40},{1,17}... | collective-permute-start | bytes 393224 | tf_op jit(solution)/shard_map/ppermute | solution.py:22
  173.2 14.1 %collective-permute-start.15 = (f32[2]{0:T(128)S(1)}, f32[2]{0:T(128)S(1)}, u32[]{:S(2)}, u32[]{:S(2)}) collective-permute-start(f32[2]{0:T(128)S(1)} %fusion.127), channel_id=1, source_target_pairs={{0,8},{8,0},{16,24},{24,16},{32,40},{40,32},{48,56},{56,48},{1,9},... | collective-permute-start | bytes 32 | tf_op jit(solution)/shard_map/ppermute | solution.py:22
  177.9 26.9 %collective-permute-start.21 = (f32[512,64]{0,1:T(8,128)S(1)}, f32[512,64]{0,1:T(8,128)S(1)}, u32[]{:S(2)}, u32[]{:S(2)}) collective-permute-start(f32[512,64]{0,1:T(8,128)S(1)} %add.384), channel_id=1, source_target_pairs={{0,32},{8,40},{16,48},{24,56},{32,0},{40,8},{48,16},{56,24},{1,33}... | collective-permute-start | bytes 393224 | tf_op jit(solution)/shard_map/ppermute | solution.py:22
  188.6 6.3 %collective-permute-start.16 = (f32[2]{0:T(128)S(1)}, f32[2]{0:T(128)S(1)}, u32[]{:S(2)}, u32[]{:S(2)}) collective-permute-start(f32[2]{0:T(128)S(1)} %fusion.133), channel_id=1, source_target_pairs={{0,16},{8,24},{16,0},{24,8},{32,48},{40,56},{48,32},{56,40},{1,17}... | collective-permute-start | bytes 32 | tf_op jit(solution)/shard_map/ppermute | solution.py:22
  194.9 9.3 %collective-permute-start.17 = (f32[2]{0:T(128)S(1)}, f32[2]{0:T(128)S(1)}, u32[]{:S(2)}, u32[]{:S(2)}) collective-permute-start(f32[2]{0:T(128)S(1)} %add.380), channel_id=1, source_target_pairs={{0,32},{8,40},{16,48},{24,56},{32,0},{40,8},{48,16},{56,24},{1,33}... | collective-permute-start | bytes 32 | tf_op jit(solution)/shard_map/ppermute | solution.py:22
  218.2 6.9 %collective-permute-start.24 = (f32[2]{0:T(128)S(1)}, f32[2]{0:T(128)S(1)}, u32[]{:S(2)}, u32[]{:S(2)}) collective-permute-start(f32[2]{0:T(128)S(1)} %fusion.132), channel_id=1, source_target_pairs={{0,4},{2,6},{4,0},{6,2},{1,5},{3,7},{5,1},{7,3},{8,12},{10,14},{12... | collective-permute-start | bytes 32 | tf_op jit(solution)/shard_map/ppermute | solution.py:22
  225.1 6.3 %collective-permute-start.25 = (f32[2]{0:T(128)S(1)}, f32[2]{0:T(128)S(1)}, u32[]{:S(2)}, u32[]{:S(2)}) collective-permute-start(f32[2]{0:T(128)S(1)} %add.390), channel_id=1, source_target_pairs={{0,128},{128,0},{256,384},{384,256},{1,129},{129,1},{257,385},{385... | collective-permute-start | bytes 32 | tf_op jit(solution)/shard_map/ppermute | solution.py:22
  231.5 9.3 %collective-permute-start.26 = (f32[2]{0:T(128)S(1)}, f32[2]{0:T(128)S(1)}, u32[]{:S(2)}, u32[]{:S(2)}) collective-permute-start(f32[2]{0:T(128)S(1)} %add.391), channel_id=1, source_target_pairs={{0,256},{128,384},{256,0},{384,128},{1,257},{129,385},{257,1},{385... | collective-permute-start | bytes 32 | tf_op jit(solution)/shard_map/ppermute | solution.py:22
  246.3 6.9 %collective-permute-start.32 = (f32[512,64]{0,1:T(8,128)S(1)}, f32[512,64]{0,1:T(8,128)S(1)}, u32[]{:S(2)}, u32[]{:S(2)}) collective-permute-start(f32[512,64]{0,1:T(8,128)S(1)} %pad_maximum_fusion.3), channel_id=1, source_target_pairs={{0,64},{64,0},{1,65},{65,1},{2,66},{66,2},{3,67},{67,3},{4,68},{68... | collective-permute-start | bytes 393224 | tf_op jit(solution)/shard_map/ppermute | solution.py:22
  253.2 26.9 %collective-permute-start.33 = (f32[512,64]{0,1:T(8,128)S(1)}, f32[512,64]{0,1:T(8,128)S(1)}, u32[]{:S(2)}, u32[]{:S(2)}) collective-permute-start(f32[512,64]{0,1:T(8,128)S(1)} %fusion.38), channel_id=1, source_target_pairs={{0,8},{8,0},{16,24},{24,16},{32,40},{40,32},{48,56},{56,48},{1,9},... | collective-permute-start | bytes 393224 | tf_op jit(solution)/shard_map/ppermute | solution.py:22
  261.0 7.3 %collective-permute-start.29 = (f32[256,32]{0,1:T(8,128)S(1)}, f32[256,32]{0,1:T(8,128)S(1)}, u32[]{:S(2)}, u32[]{:S(2)}) collective-permute-start(f32[256,32]{0,1:T(8,128)S(1)} %add.400), channel_id=1, source_target_pairs={{0,4},{2,6},{4,0},{6,2},{1,5},{3,7},{5,1},{7,3},{8,12},{10,14},{12... | collective-permute-start | bytes 98312 | tf_op jit(solution)/shard_map/ppermute | solution.py:22
  268.3 6.7 %collective-permute-start.30 = (f32[256,32]{0,1:T(8,128)S(1)}, f32[256,32]{0,1:T(8,128)S(1)}, u32[]{:S(2)}, u32[]{:S(2)}) collective-permute-start(f32[256,32]{0,1:T(8,128)S(1)} %add.401), channel_id=1, source_target_pairs={{0,128},{128,0},{256,384},{384,256},{1,129},{129,1},{257,385},{385... | collective-permute-start | bytes 98312 | tf_op jit(solution)/shard_map/ppermute | solution.py:22
  275.0 9.7 %collective-permute-start.31 = (f32[256,32]{0,1:T(8,128)S(1)}, f32[256,32]{0,1:T(8,128)S(1)}, u32[]{:S(2)}, u32[]{:S(2)}) collective-permute-start(f32[256,32]{0,1:T(8,128)S(1)} %add.402), channel_id=1, source_target_pairs={{0,256},{128,384},{256,0},{384,128},{1,257},{129,385},{257,1},{385... | collective-permute-start | bytes 98312 | tf_op jit(solution)/shard_map/ppermute | solution.py:22
  280.2 10.0 %collective-permute-start.34 = (f32[512,64]{0,1:T(8,128)S(1)}, f32[512,64]{0,1:T(8,128)S(1)}, u32[]{:S(2)}, u32[]{:S(2)}) collective-permute-start(f32[512,64]{0,1:T(8,128)S(1)} %add.405), channel_id=1, source_target_pairs={{0,16},{8,24},{16,0},{24,8},{32,48},{40,56},{48,32},{56,40},{1,17}... | collective-permute-start | bytes 393224 | tf_op jit(solution)/shard_map/ppermute | solution.py:22
  290.2 10.8 %collective-permute-start.35 = (f32[512,64]{0,1:T(8,128)S(1)}, f32[512,64]{0,1:T(8,128)S(1)}, u32[]{:S(2)}, u32[]{:S(2)}) collective-permute-start(f32[512,64]{0,1:T(8,128)S(1)} %add.406), channel_id=1, source_target_pairs={{0,32},{8,40},{16,48},{24,56},{32,0},{40,8},{48,16},{56,24},{1,33}... | collective-permute-start | bytes 393224 | tf_op jit(solution)/shard_map/ppermute | solution.py:22
  306.3 26.4 %collective-permute-start.45 = (f32[512,64]{0,1:T(8,128)S(1)}, f32[512,64]{0,1:T(8,128)S(1)}, u32[]{:S(2)}, u32[]{:S(2)}) collective-permute-start(f32[512,64]{0,1:T(8,128)S(1)} %pad_maximum_fusion.4), channel_id=1, source_target_pairs={{0,64},{64,0},{1,65},{65,1},{2,66},{66,2},{3,67},{67,3},{4,68},{68... | collective-permute-start | bytes 393224 | tf_op jit(solution)/shard_map/ppermute | solution.py:22
  314.1 7.3 %collective-permute-start.38 = (f32[256,32]{0,1:T(8,128)S(1)}, f32[256,32]{0,1:T(8,128)S(1)}, u32[]{:S(2)}, u32[]{:S(2)}) collective-permute-start(f32[256,32]{0,1:T(8,128)S(1)} %add.411), channel_id=1, source_target_pairs={{0,4},{2,6},{4,0},{6,2},{1,5},{3,7},{5,1},{7,3},{8,12},{10,14},{12... | collective-permute-start | bytes 98312 | tf_op jit(solution)/shard_map/ppermute | solution.py:22
  321.4 6.7 %collective-permute-start.39 = (f32[256,32]{0,1:T(8,128)S(1)}, f32[256,32]{0,1:T(8,128)S(1)}, u32[]{:S(2)}, u32[]{:S(2)}) collective-permute-start(f32[256,32]{0,1:T(8,128)S(1)} %add.412), channel_id=1, source_target_pairs={{0,128},{128,0},{256,384},{384,256},{1,129},{129,1},{257,385},{385... | collective-permute-start | bytes 98312 | tf_op jit(solution)/shard_map/ppermute | solution.py:22
  328.1 9.7 %collective-permute-start.40 = (f32[256,32]{0,1:T(8,128)S(1)}, f32[256,32]{0,1:T(8,128)S(1)}, u32[]{:S(2)}, u32[]{:S(2)}) collective-permute-start(f32[256,32]{0,1:T(8,128)S(1)} %add.413), channel_id=1, source_target_pairs={{0,256},{128,384},{256,0},{384,128},{1,257},{129,385},{257,1},{385... | collective-permute-start | bytes 98312 | tf_op jit(solution)/shard_map/ppermute | solution.py:22
  332.7 11.9 %collective-permute-start.46 = (f32[512,64]{0,1:T(8,128)S(1)}, f32[512,64]{0,1:T(8,128)S(1)}, u32[]{:S(2)}, u32[]{:S(2)}) collective-permute-start(f32[512,64]{0,1:T(8,128)S(1)} %fusion.37), channel_id=1, source_target_pairs={{0,8},{8,0},{16,24},{24,16},{32,40},{40,32},{48,56},{56,48},{1,9},... | collective-permute-start | bytes 393224 | tf_op jit(solution)/shard_map/ppermute | solution.py:22
  340.4 6.7 %collective-permute-start.41 = (f32[2]{0:T(128)S(1)}, f32[2]{0:T(128)S(1)}, u32[]{:S(2)}, u32[]{:S(2)}) collective-permute-start(f32[2]{0:T(128)S(1)} %pad_maximum_fusion.9), channel_id=1, source_target_pairs={{0,64},{64,0},{1,65},{65,1},{2,66},{66,2},{3,67},{67,3},{4,68},{68... | collective-permute-start | bytes 32 | tf_op jit(solution)/shard_map/ppermute | solution.py:22
  344.7 10.0 %collective-permute-start.47 = (f32[512,64]{0,1:T(8,128)S(1)}, f32[512,64]{0,1:T(8,128)S(1)}, u32[]{:S(2)}, u32[]{:S(2)}) collective-permute-start(f32[512,64]{0,1:T(8,128)S(1)} %add.421), channel_id=1, source_target_pairs={{0,16},{8,24},{16,0},{24,8},{32,48},{40,56},{48,32},{56,40},{1,17}... | collective-permute-start | bytes 393224 | tf_op jit(solution)/shard_map/ppermute | solution.py:22
  348.4 8.2 %collective-permute-start.42 = (f32[2]{0:T(128)S(1)}, f32[2]{0:T(128)S(1)}, u32[]{:S(2)}, u32[]{:S(2)}) collective-permute-start(f32[2]{0:T(128)S(1)} %fusion.125), channel_id=1, source_target_pairs={{0,8},{8,0},{16,24},{24,16},{32,40},{40,32},{48,56},{56,48},{1,9},... | collective-permute-start | bytes 32 | tf_op jit(solution)/shard_map/ppermute | solution.py:22
  354.7 19.5 %collective-permute-start.48 = (f32[512,64]{0,1:T(8,128)S(1)}, f32[512,64]{0,1:T(8,128)S(1)}, u32[]{:S(2)}, u32[]{:S(2)}) collective-permute-start(f32[512,64]{0,1:T(8,128)S(1)} %add.422), channel_id=1, source_target_pairs={{0,32},{8,40},{16,48},{24,56},{32,0},{40,8},{48,16},{56,24},{1,33}... | collective-permute-start | bytes 393224 | tf_op jit(solution)/shard_map/ppermute | solution.py:22
  357.9 6.3 %collective-permute-start.43 = (f32[2]{0:T(128)S(1)}, f32[2]{0:T(128)S(1)}, u32[]{:S(2)}, u32[]{:S(2)}) collective-permute-start(f32[2]{0:T(128)S(1)} %fusion.131), channel_id=1, source_target_pairs={{0,16},{8,24},{16,0},{24,8},{32,48},{40,56},{48,32},{56,40},{1,17}... | collective-permute-start | bytes 32 | tf_op jit(solution)/shard_map/ppermute | solution.py:22
  364.3 9.3 %collective-permute-start.44 = (f32[2]{0:T(128)S(1)}, f32[2]{0:T(128)S(1)}, u32[]{:S(2)}, u32[]{:S(2)}) collective-permute-start(f32[2]{0:T(128)S(1)} %add.418), channel_id=1, source_target_pairs={{0,32},{8,40},{16,48},{24,56},{32,0},{40,8},{48,16},{56,24},{1,33}... | collective-permute-start | bytes 32 | tf_op jit(solution)/shard_map/ppermute | solution.py:22
  387.5 6.9 %collective-permute-start.51 = (f32[2]{0:T(128)S(1)}, f32[2]{0:T(128)S(1)}, u32[]{:S(2)}, u32[]{:S(2)}) collective-permute-start(f32[2]{0:T(128)S(1)} %fusion.130), channel_id=1, source_target_pairs={{0,4},{2,6},{4,0},{6,2},{1,5},{3,7},{5,1},{7,3},{8,12},{10,14},{12... | collective-permute-start | bytes 32 | tf_op jit(solution)/shard_map/ppermute | solution.py:22
  394.5 6.3 %collective-permute-start.52 = (f32[2]{0:T(128)S(1)}, f32[2]{0:T(128)S(1)}, u32[]{:S(2)}, u32[]{:S(2)}) collective-permute-start(f32[2]{0:T(128)S(1)} %add.428), channel_id=1, source_target_pairs={{0,128},{128,0},{256,384},{384,256},{1,129},{129,1},{257,385},{385... | collective-permute-start | bytes 32 | tf_op jit(solution)/shard_map/ppermute | solution.py:22
  400.8 9.3 %collective-permute-start.53 = (f32[2]{0:T(128)S(1)}, f32[2]{0:T(128)S(1)}, u32[]{:S(2)}, u32[]{:S(2)}) collective-permute-start(f32[2]{0:T(128)S(1)} %add.429), channel_id=1, source_target_pairs={{0,256},{128,384},{256,0},{384,128},{1,257},{129,385},{257,1},{385... | collective-permute-start | bytes 32 | tf_op jit(solution)/shard_map/ppermute | solution.py:22
  415.6 6.9 %collective-permute-start.59 = (f32[512,64]{0,1:T(8,128)S(1)}, f32[512,64]{0,1:T(8,128)S(1)}, u32[]{:S(2)}, u32[]{:S(2)}) collective-permute-start(f32[512,64]{0,1:T(8,128)S(1)} %pad_maximum_fusion.5), channel_id=1, source_target_pairs={{0,64},{64,0},{1,65},{65,1},{2,66},{66,2},{3,67},{67,3},{4,68},{68... | collective-permute-start | bytes 393224 | tf_op jit(solution)/shard_map/ppermute | solution.py:22
  422.5 26.4 %collective-permute-start.60 = (f32[512,64]{0,1:T(8,128)S(1)}, f32[512,64]{0,1:T(8,128)S(1)}, u32[]{:S(2)}, u32[]{:S(2)}) collective-permute-start(f32[512,64]{0,1:T(8,128)S(1)} %fusion.36), channel_id=1, source_target_pairs={{0,8},{8,0},{16,24},{24,16},{32,40},{40,32},{48,56},{56,48},{1,9},... | collective-permute-start | bytes 393224 | tf_op jit(solution)/shard_map/ppermute | solution.py:22
  430.3 7.3 %collective-permute-start.56 = (f32[256,32]{0,1:T(8,128)S(1)}, f32[256,32]{0,1:T(8,128)S(1)}, u32[]{:S(2)}, u32[]{:S(2)}) collective-permute-start(f32[256,32]{0,1:T(8,128)S(1)} %add.438), channel_id=1, source_target_pairs={{0,4},{2,6},{4,0},{6,2},{1,5},{3,7},{5,1},{7,3},{8,12},{10,14},{12... | collective-permute-start | bytes 98312 | tf_op jit(solution)/shard_map/ppermute | solution.py:22
  437.6 7.0 %collective-permute-start.57 = (f32[256,32]{0,1:T(8,128)S(1)}, f32[256,32]{0,1:T(8,128)S(1)}, u32[]{:S(2)}, u32[]{:S(2)}) collective-permute-start(f32[256,32]{0,1:T(8,128)S(1)} %add.439), channel_id=1, source_target_pairs={{0,128},{128,0},{256,384},{384,256},{1,129},{129,1},{257,385},{385... | collective-permute-start | bytes 98312 | tf_op jit(solution)/shard_map/ppermute | solution.py:22
  444.6 9.7 %collective-permute-start.58 = (f32[256,32]{0,1:T(8,128)S(1)}, f32[256,32]{0,1:T(8,128)S(1)}, u32[]{:S(2)}, u32[]{:S(2)}) collective-permute-start(f32[256,32]{0,1:T(8,128)S(1)} %add.440), channel_id=1, source_target_pairs={{0,256},{128,384},{256,0},{384,128},{1,257},{129,385},{257,1},{385... | collective-permute-start | bytes 98312 | tf_op jit(solution)/shard_map/ppermute | solution.py:22
  448.9 7.8 %collective-permute-start.61 = (f32[512,64]{0,1:T(8,128)S(1)}, f32[512,64]{0,1:T(8,128)S(1)}, u32[]{:S(2)}, u32[]{:S(2)}) collective-permute-start(f32[512,64]{0,1:T(8,128)S(1)} %add.443), channel_id=1, source_target_pairs={{0,16},{8,24},{16,0},{24,8},{32,48},{40,56},{48,32},{56,40},{1,17}... | collective-permute-start | bytes 393224 | tf_op jit(solution)/shard_map/ppermute | solution.py:22
  456.7 13.6 %collective-permute-start.62 = (f32[512,64]{0,1:T(8,128)S(1)}, f32[512,64]{0,1:T(8,128)S(1)}, u32[]{:S(2)}, u32[]{:S(2)}) collective-permute-start(f32[512,64]{0,1:T(8,128)S(1)} %add.444), channel_id=1, source_target_pairs={{0,32},{8,40},{16,48},{24,56},{32,0},{40,8},{48,16},{56,24},{1,33}... | collective-permute-start | bytes 393224 | tf_op jit(solution)/shard_map/ppermute | solution.py:22
  475.6 26.6 %collective-permute-start.72 = (f32[512,64]{0,1:T(8,128)S(1)}, f32[512,64]{0,1:T(8,128)S(1)}, u32[]{:S(2)}, u32[]{:S(2)}) collective-permute-start(f32[512,64]{0,1:T(8,128)S(1)} %pad_maximum_fusion.6), channel_id=1, source_target_pairs={{0,64},{64,0},{1,65},{65,1},{2,66},{66,2},{3,67},{67,3},{4,68},{68... | collective-permute-start | bytes 393224 | tf_op jit(solution)/shard_map/ppermute | solution.py:22
  483.4 7.3 %collective-permute-start.65 = (f32[256,32]{0,1:T(8,128)S(1)}, f32[256,32]{0,1:T(8,128)S(1)}, u32[]{:S(2)}, u32[]{:S(2)}) collective-permute-start(f32[256,32]{0,1:T(8,128)S(1)} %add.449), channel_id=1, source_target_pairs={{0,4},{2,6},{4,0},{6,2},{1,5},{3,7},{5,1},{7,3},{8,12},{10,14},{12... | collective-permute-start | bytes 98312 | tf_op jit(solution)/shard_map/ppermute | solution.py:22
  490.7 6.7 %collective-permute-start.66 = (f32[256,32]{0,1:T(8,128)S(1)}, f32[256,32]{0,1:T(8,128)S(1)}, u32[]{:S(2)}, u32[]{:S(2)}) collective-permute-start(f32[256,32]{0,1:T(8,128)S(1)} %add.450), channel_id=1, source_target_pairs={{0,128},{128,0},{256,384},{384,256},{1,129},{129,1},{257,385},{385... | collective-permute-start | bytes 98312 | tf_op jit(solution)/shard_map/ppermute | solution.py:22
  497.4 10.0 %collective-permute-start.67 = (f32[256,32]{0,1:T(8,128)S(1)}, f32[256,32]{0,1:T(8,128)S(1)}, u32[]{:S(2)}, u32[]{:S(2)}) collective-permute-start(f32[256,32]{0,1:T(8,128)S(1)} %add.451), channel_id=1, source_target_pairs={{0,256},{128,384},{256,0},{384,128},{1,257},{129,385},{257,1},{385... | collective-permute-start | bytes 98312 | tf_op jit(solution)/shard_map/ppermute | solution.py:22
  502.3 11.4 %collective-permute-start.73 = (f32[512,64]{0,1:T(8,128)S(1)}, f32[512,64]{0,1:T(8,128)S(1)}, u32[]{:S(2)}, u32[]{:S(2)}) collective-permute-start(f32[512,64]{0,1:T(8,128)S(1)} %fusion.35), channel_id=1, source_target_pairs={{0,8},{8,0},{16,24},{24,16},{32,40},{40,32},{48,56},{56,48},{1,9},... | collective-permute-start | bytes 393224 | tf_op jit(solution)/shard_map/ppermute | solution.py:22
  510.1 6.4 %collective-permute-start.68 = (f32[2]{0:T(128)S(1)}, f32[2]{0:T(128)S(1)}, u32[]{:S(2)}, u32[]{:S(2)}) collective-permute-start(f32[2]{0:T(128)S(1)} %pad_maximum_fusion.11), channel_id=1, source_target_pairs={{0,64},{64,0},{1,65},{65,1},{2,66},{66,2},{3,67},{67,3},{4,68},{68... | collective-permute-start | bytes 32 | tf_op jit(solution)/shard_map/ppermute | solution.py:22
  513.7 9.2 %collective-permute-start.74 = (f32[512,64]{0,1:T(8,128)S(1)}, f32[512,64]{0,1:T(8,128)S(1)}, u32[]{:S(2)}, u32[]{:S(2)}) collective-permute-start(f32[512,64]{0,1:T(8,128)S(1)} %add.459), channel_id=1, source_target_pairs={{0,16},{8,24},{16,0},{24,8},{32,48},{40,56},{48,32},{56,40},{1,17}... | collective-permute-start | bytes 393224 | tf_op jit(solution)/shard_map/ppermute | solution.py:22
  517.8 14.3 %collective-permute-start.69 = (f32[2]{0:T(128)S(1)}, f32[2]{0:T(128)S(1)}, u32[]{:S(2)}, u32[]{:S(2)}) collective-permute-start(f32[2]{0:T(128)S(1)} %fusion.123), channel_id=1, source_target_pairs={{0,8},{8,0},{16,24},{24,16},{32,40},{40,32},{48,56},{56,48},{1,9},... | collective-permute-start | bytes 32 | tf_op jit(solution)/shard_map/ppermute | solution.py:22
  522.9 26.8 %collective-permute-start.75 = (f32[512,64]{0,1:T(8,128)S(1)}, f32[512,64]{0,1:T(8,128)S(1)}, u32[]{:S(2)}, u32[]{:S(2)}) collective-permute-start(f32[512,64]{0,1:T(8,128)S(1)} %add.460), channel_id=1, source_target_pairs={{0,32},{8,40},{16,48},{24,56},{32,0},{40,8},{48,16},{56,24},{1,33}... | collective-permute-start | bytes 393224 | tf_op jit(solution)/shard_map/ppermute | solution.py:22
  533.4 6.3 %collective-permute-start.70 = (f32[2]{0:T(128)S(1)}, f32[2]{0:T(128)S(1)}, u32[]{:S(2)}, u32[]{:S(2)}) collective-permute-start(f32[2]{0:T(128)S(1)} %fusion.129), channel_id=1, source_target_pairs={{0,16},{8,24},{16,0},{24,8},{32,48},{40,56},{48,32},{56,40},{1,17}... | collective-permute-start | bytes 32 | tf_op jit(solution)/shard_map/ppermute | solution.py:22
  539.8 9.3 %collective-permute-start.71 = (f32[2]{0:T(128)S(1)}, f32[2]{0:T(128)S(1)}, u32[]{:S(2)}, u32[]{:S(2)}) collective-permute-start(f32[2]{0:T(128)S(1)} %add.456), channel_id=1, source_target_pairs={{0,32},{8,40},{16,48},{24,56},{32,0},{40,8},{48,16},{56,24},{1,33}... | collective-permute-start | bytes 32 | tf_op jit(solution)/shard_map/ppermute | solution.py:22
  563.0 6.9 %collective-permute-start.78 = (f32[2]{0:T(128)S(1)}, f32[2]{0:T(128)S(1)}, u32[]{:S(2)}, u32[]{:S(2)}) collective-permute-start(f32[2]{0:T(128)S(1)} %fusion.128), channel_id=1, source_target_pairs={{0,4},{2,6},{4,0},{6,2},{1,5},{3,7},{5,1},{7,3},{8,12},{10,14},{12... | collective-permute-start | bytes 32 | tf_op jit(solution)/shard_map/ppermute | solution.py:22
  576.3 9.3 %collective-permute-start.80 = (f32[2]{0:T(128)S(1)}, f32[2]{0:T(128)S(1)}, u32[]{:S(2)}, u32[]{:S(2)}) collective-permute-start(f32[2]{0:T(128)S(1)} %add.467), channel_id=1, source_target_pairs={{0,256},{128,384},{256,0},{384,128},{1,257},{129,385},{257,1},{385... | collective-permute-start | bytes 32 | tf_op jit(solution)/shard_map/ppermute | solution.py:22
  (21 other events, 120.8 us)
